TPU v7x, 256 devices: a whole 4x4x8 slice. The times are simulated.
256 devices in a mesh: kv: 8 (over z), blk: 32 (over y, x, core).
Axes of the slice: x: 4, y: 4, z: 8, core: 2. Of those that a mesh axis runs over, the one named last changes fastest.
Arguments:
- embeds: bfloat16 [1, 256, 3072], P(None, None, 'blk'), may hold values from -40 to 40
- attn_norm: float32 [3072], P('blk'), may hold values from 0.25 to 1.75
- query_key_value_weight: bfloat16 [3072, 5120], P('blk', 'kv'), may hold values from -0.109375 to 0.109375
- w_out: bfloat16 [3072, 3072], P('kv', 'blk'), may hold values from -0.109375 to 0.109375
- mlp_norm: float32 [3072], P('blk'), may hold values from 0.25 to 1.75
- w_gate: bfloat16 [3072, 8192], P('blk', 'kv'), may hold values from -0.109375 to 0.109375
- w_up: bfloat16 [3072, 8192], P('blk', 'kv'), may hold values from -0.109375 to 0.109375
- w_down: bfloat16 [8192, 3072], P('kv', 'blk'), may hold values from -0.0625 to 0.0625
- prompt_key_slots: bfloat16 [256, 8, 128, 128], P('blk', 'kv'), may hold values from -210 to 210
- prompt_value_slots: bfloat16 [256, 8, 128, 128], P('blk', 'kv'), may hold values from -6 to 6
- generated_keys: bfloat16 [256, 8, 127, 128], P('blk', 'kv'), may hold values from -10 to 10
- generated_values: bfloat16 [256, 8, 127, 128], P('blk', 'kv'), may hold values from -6 to 6
- parents: int32 [1, 256], P(None, 'blk'), may hold values from 0 to 7
- prompt_length: int32 [32], replicated, may hold values from 1024 to 8192
- tenant_bounds: int32 [5], replicated, may hold values from 0 to 32, as said below
- slot_table: int32 [256], P('blk'), may hold values from 0 to 256, as said below
Outputs:
- hidden_out: float32 [1, 256, 3072], P(None, None, 'blk')
- keys_out: bfloat16 [256, 8, 128, 128], P('blk', 'kv')
- values_out: bfloat16 [256, 8, 128, 128], P('blk', 'kv')
Inputs may be any that keep to these rules, and one draw needn't show every extreme that they name: parents[s, b] is the beam, among the 8 beams of b's request, whose cache beam b continues at step s. tenant_bounds[0] = 0 and tenant_bounds[4] = 32, strictly rising. `slot_table`: with L_t the largest prompt_length of tenant t's requests, every block j below ceil(L_t / 128) of every tenant t stands in exactly one slot as t * 64 + j, no other block stands anywhere, and 256 marks an empty slot.
All inputs are finite; a program needn't handle non-finite values.
Results may differ from a plain program's by a relative error of at most 0.012.
The roundings to bfloat16 on the way count: a program that leaves them out, or rounds other values in their place, can miss the bound.
Values may be sent and summed in bfloat16 or wider, within the bound.
No kernel may reach another device: no remote copies, remote signals or barrier semaphores. Data moves between devices by JAX's collectives and lax.ppermute only.
A program may use at most 64 MiB of HBM per device.

v0:
```python
import math
import jax
import jax.numpy as jnp
from jax import lax
from jax.sharding import PartitionSpec as P

MODEL_WIDTH = 3072
QUERY_HEADS = 24
KEY_VALUE_HEADS = 8
HEAD_WIDTH = 128
REQUEST_BEAMS = 8
TENANT_COUNT = 4
BLOCK_POSITIONS = 128
PROMPT_BLOCKS = 64
EARLIER_TOKENS = 127
DECODE_STEPS = 1
masked_score = -1e30


def exchange(value, axis, bit):
    count = lax.axis_size(axis)
    return lax.ppermute(value, axis, [(i, i ^ 1 << bit) for i in range(count)])


def butterfly_sum(value, axis):
    count = lax.axis_size(axis)
    if count & count - 1:
        return lax.psum(value, axis)
    for bit in range(count.bit_length() - 1):
        value = value + exchange(value, axis, bit)
    return value


def scatter_sum(value, axis):
    count = lax.axis_size(axis)
    pieces = value.reshape((count, value.shape[0] // count) + value.shape[1:])
    return jnp.sum(lax.all_to_all(pieces, axis, 0, 0, tiled=False), axis=0)


def rotate(values, angles):
    half = values.shape[-1] // 2
    first = values[..., :half]
    second = values[..., half:]
    cosine = jnp.cos(angles)
    sine = jnp.sin(angles)
    return jnp.concatenate(
        [first * cosine - second * sine, second * cosine + first * sine], axis=-1
    )


def angles_for(positions, head_size):
    half = head_size // 2
    freq = jnp.exp(jnp.arange(half, dtype=jnp.float32) * (-math.log(500000.0) / half))
    return positions.astype(jnp.float32)[:, None] * freq[None, :]


def across_heads(partial_value):
    return butterfly_sum(partial_value, "kv")


def body(
    embeds,
    attn_norm,
    query_key_value_weight,
    w_out,
    mlp_norm,
    w_gate,
    w_up,
    w_down,
    prompt_key_slots,
    prompt_value_slots,
    generated_keys,
    generated_values,
    parents,
    prompt_length,
    tenant_bounds,
    slot_table,
):
    blocks = lax.axis_size("blk")
    my_index = lax.axis_index("blk")
    all_rows = embeds.shape[1]
    own_rows = all_rows // blocks
    heads_kv = prompt_key_slots.shape[1]
    slots_here = prompt_key_slots.shape[0]
    keys_here = slots_here * BLOCK_POSITIONS
    group_queries = QUERY_HEADS // KEY_VALUE_HEADS
    col_width = group_queries + 2
    score_scale = 1.0 / math.sqrt(HEAD_WIDTH)
    unit_count = w_gate.shape[1]
    beam_req = jnp.arange(all_rows, dtype=jnp.int32) // REQUEST_BEAMS
    tenant_beam = jnp.sum(
        (beam_req[:, None] >= tenant_bounds[None, 1:TENANT_COUNT]).astype(jnp.int32), axis=1
    )
    length_beam = jnp.repeat(prompt_length, REQUEST_BEAMS)
    slot_tenant = jnp.repeat(slot_table // PROMPT_BLOCKS, BLOCK_POSITIONS)
    slot_pos = jnp.repeat(slot_table % PROMPT_BLOCKS * BLOCK_POSITIONS, BLOCK_POSITIONS) + jnp.tile(
        jnp.arange(BLOCK_POSITIONS, dtype=jnp.int32), slots_here
    )
    visible = (tenant_beam[:, None] == slot_tenant[None, :]) & (
        slot_pos[None, :] < length_beam[:, None]
    )
    prompt_mask = visible[None, :, None, :]
    keys_flat = prompt_key_slots.transpose(1, 0, 2, 3).reshape(heads_kv, keys_here, HEAD_WIDTH)
    values_flat = prompt_value_slots.transpose(1, 0, 2, 3).reshape(heads_kv, keys_here, HEAD_WIDTH)
    local_beam = jnp.arange(own_rows, dtype=jnp.int32)
    base_rows = local_beam // REQUEST_BEAMS * REQUEST_BEAMS
    trailing_zeros = jnp.zeros((own_rows, heads_kv, DECODE_STEPS, HEAD_WIDTH), jnp.bfloat16)
    cached_key_rows = jnp.concatenate([generated_keys, trailing_zeros], axis=2)
    cached_value_rows = jnp.concatenate([generated_values, trailing_zeros], axis=2)
    gen_pos = jnp.arange(EARLIER_TOKENS + DECODE_STEPS, dtype=jnp.int32)
    w_both = jnp.concatenate([w_gate, w_up], axis=1)
    residual = embeds[0].astype(jnp.float32)
    squares = jnp.sum(residual * residual, axis=1)
    normed = (residual * attn_norm).astype(jnp.bfloat16)
    partial_value = jnp.dot(normed, query_key_value_weight, preferred_element_type=jnp.float32)
    own_value = scatter_sum(jnp.concatenate([partial_value, squares[:, None]], axis=1), "blk")
    inverse = lax.rsqrt(own_value[:, -1] / MODEL_WIDTH + 1e-05)
    own_proj = (own_value[:, :-1] * inverse[:, None]).reshape(
        own_rows, heads_kv, col_width, HEAD_WIDTH
    )
    own_length = lax.dynamic_slice_in_dim(length_beam, my_index * own_rows, own_rows, 0)
    own_angle = angles_for(own_length + EARLIER_TOKENS + 0, HEAD_WIDTH)
    own_queries = rotate(own_proj[:, :, :group_queries], own_angle[:, None, None, :]).astype(
        jnp.bfloat16
    )
    query_rows = lax.all_gather(own_queries, "blk", axis=0, tiled=True)
    new_key = rotate(own_proj[:, :, group_queries], own_angle[:, None, :]).astype(jnp.bfloat16)
    new_value = own_proj[:, :, group_queries + 1].astype(jnp.bfloat16)
    parent_rows = base_rows + parents[0]
    cached_key_rows = (
        jnp.take(cached_key_rows, parent_rows, axis=0).at[:, :, EARLIER_TOKENS].set(new_key)
    )
    cached_value_rows = (
        jnp.take(cached_value_rows, parent_rows, axis=0).at[:, :, EARLIER_TOKENS].set(new_value)
    )
    grouped = query_rows.transpose(1, 0, 2, 3).reshape(
        heads_kv, all_rows * group_queries, HEAD_WIDTH
    )
    scores = jnp.einsum("kqd,knd->kqn", grouped, keys_flat, preferred_element_type=jnp.float32)
    scores = scores.reshape(heads_kv, all_rows, group_queries, keys_here) * score_scale
    top_score = jnp.max(jnp.where(prompt_mask, scores, masked_score), axis=3)
    weights = jnp.where(prompt_mask, jnp.exp(scores - top_score[..., None]), 0.0)
    total_mass = jnp.sum(weights, axis=3)
    flat_weights = weights.reshape(heads_kv, all_rows * group_queries, keys_here).astype(
        jnp.bfloat16
    )
    summed = jnp.einsum(
        "kqn,knd->kqd", flat_weights, values_flat, preferred_element_type=jnp.float32
    )
    summed = summed.reshape(heads_kv, all_rows, group_queries, HEAD_WIDTH)
    packed = jnp.concatenate([summed, top_score[..., None], total_mass[..., None]], axis=3)
    packed = packed.transpose(1, 0, 2, 3).reshape(
        blocks, own_rows, heads_kv, group_queries, HEAD_WIDTH + 2
    )
    parts = lax.all_to_all(packed, "blk", 0, 0, tiled=False)
    part_top = parts[..., HEAD_WIDTH]
    prompt_top = jnp.max(part_top, axis=0)
    part_factor = jnp.exp(part_top - prompt_top[None])
    prompt_mass = jnp.sum(parts[..., HEAD_WIDTH + 1] * part_factor, axis=0)
    prompt_sum = jnp.sum(parts[..., :HEAD_WIDTH] * part_factor[..., None], axis=0)
    prompt_top = prompt_top.transpose(1, 0, 2)
    prompt_mass = prompt_mass.transpose(1, 0, 2)
    prompt_sum = prompt_sum.transpose(1, 0, 2, 3)
    gen_scores = (
        jnp.einsum(
            "bkgd,bknd->kbgn", own_queries, cached_key_rows, preferred_element_type=jnp.float32
        )
        * score_scale
    )
    live = (gen_pos <= EARLIER_TOKENS)[None, None, None, :]
    gen_top = jnp.max(jnp.where(live, gen_scores, masked_score), axis=3)
    best = jnp.maximum(prompt_top, gen_top)
    gen_weights = jnp.where(live, jnp.exp(gen_scores - best[..., None]), 0.0)
    shift = jnp.exp(prompt_top - best)
    full_mass = prompt_mass * shift + jnp.sum(gen_weights, axis=3)
    gen_sum = jnp.einsum(
        "kbgn,bknd->kbgd",
        gen_weights.astype(jnp.bfloat16),
        cached_value_rows,
        preferred_element_type=jnp.float32,
    )
    attended_output = (prompt_sum * shift[..., None] + gen_sum) / full_mass[..., None]
    heads_out = (
        attended_output.transpose(1, 0, 2, 3)
        .reshape(own_rows, heads_kv * group_queries * HEAD_WIDTH)
        .astype(jnp.bfloat16)
    )
    head_part = jnp.dot(
        lax.all_gather(heads_out, "blk", axis=0, tiled=True),
        w_out,
        preferred_element_type=jnp.float32,
    )
    after_attn = residual + across_heads(head_part)
    squares2 = jnp.sum(after_attn * after_attn, axis=1)
    normed2 = (after_attn * mlp_norm).astype(jnp.bfloat16)
    mixed = scatter_sum(
        jnp.concatenate(
            [jnp.dot(normed2, w_both, preferred_element_type=jnp.float32), squares2[:, None]],
            axis=1,
        ),
        "blk",
    )
    own_inverse = lax.rsqrt(mixed[:, -1] / MODEL_WIDTH + 1e-05)
    gate = mixed[:, :unit_count] * own_inverse[:, None]
    upper = mixed[:, unit_count : 2 * unit_count] * own_inverse[:, None]
    hidden = (jax.nn.silu(gate) * upper).astype(jnp.bfloat16)
    ff_part = jnp.dot(
        lax.all_gather(hidden, "blk", axis=0, tiled=True),
        w_down,
        preferred_element_type=jnp.float32,
    )
    outputs = [after_attn + across_heads(ff_part)]
    return (jnp.stack(outputs), cached_key_rows, cached_value_rows)


def solution(mesh):
    in_specs = (
        P(None, None, "blk"),
        P("blk"),
        P("blk", "kv"),
        P("kv", "blk"),
        P("blk"),
        P("blk", "kv"),
        P("blk", "kv"),
        P("kv", "blk"),
        P("blk", "kv", None, None),
        P("blk", "kv", None, None),
        P("blk", "kv", None, None),
        P("blk", "kv", None, None),
        P(None, "blk"),
        P(),
        P(),
        P("blk"),
    )
    out_specs = (P(None, None, "blk"), P("blk", "kv", None, None), P("blk", "kv", None, None))
    return jax.shard_map(body, mesh=mesh, in_specs=in_specs, out_specs=out_specs, check_vma=False)
```

profile of v0, /device:TPU:2, one launch (start us, length us, event | category | flops | bytes accessed | tf_op | source)
XLA Modules:
  0.0 210.3 jit_solution(3467085731439705462)
XLA Ops:
  0.7 1.0 copy.159
  1.7 0.8 fusion.23
  2.5 0.2 concatenate.90
  2.7 1.1 fusion.21
  3.9 0.9 pad_maximum_fusion.1
  4.8 7.6 %all-to-all-start = ((f32[32,8,641]{2,1,0:T(8,128)}), f32[32,8,641]{2,1,0:T(8,128)S(1)}, u32[]{:S(2)}, u32[]{:S(2)}) async-start(f32[32,8,641]{2,1,0:T(8,128)} %pad_maximum_fusion.1), calls=%async_computation | async-start | bytes 1572864 | tf_op jit(solution)/shard_map/all_to_all | solution.py:37
  12.6 0.1 lt.33
  13.0 0.1 multiply_cosine_fusion.1
  13.3 0.6 gather_fusion
  13.9 0.6 gather_fusion.1
  14.5 0.1 convert_reduce_fusion
  14.6 1.0 compare_and_fusion
  15.5 0.9 bitcast_select_fusion.1
  16.4 9.3 %all-to-all-done = f32[32,8,641]{2,1,0:T(8,128)S(1)} async-done(((f32[32,8,641]{2,1,0:T(8,128)}), f32[32,8,641]{2,1,0:T(8,128)S(1)}, u32[]{:S(2)}, u32[]{:S(2)}) %all-to-all-start) | async-done | bytes 656416 | tf_op jit(solution)/shard_map/all_to_all | solution.py:37
  25.8 0.1 fusion.53
  26.2 22.9 %all_gather.9 = bf16[256,1,3,128]{3,0,2,1:T(8,128)(2,1)S(1)} all-gather(bf16[8,1,3,128]{3,0,2,1:T(8,128)(2,1)S(1)} %pad_maximum_fusion.2), channel_id=1, replica_groups=mesh['kv'=8,'blk'=32] {'blk'}, dimensions={0}, use_global_device_ids=true | all-gather | bytes 202752 | tf_op jit(solution)/shard_map/all_gather | solution.py:126
  49.0 1.8 select_reduce_fusion
  50.8 0.1 concatenate.75
  50.9 3.1 %fusion.2 = (bf16[32,8,3,1024]{3,1,0,2:T(8,128)(2,1)}, f32[256,3]{0,1:T(4,128)S(1)}) fusion(f32[256,3,1024]{2,0,1:T(8,128)S(1)} %get-tuple-element.71, f32[256,3]{0,1:T(4,128)S(1)} %get-tuple-element.70, pred[256,1024]{1,0:T(8,128)(4,1)} %compare_and_fusion), kind=kLoop, calls=%fused_computation.8 | loop fusion | flops 3931392 | bytes 4986880 | tf_op jit(solution)/shard_map/reshape.462
  54.0 0.1 concatenate.76
  54.1 0.6 copy.163
  54.7 0.6 copy.162
  55.4 2.0 fusion.5
  57.4 1.1 maximum_bitcast_fusion
  58.5 5.7 %all-to-all-start.1 = ((f32[32,8,1,3,130]{4,1,3,2,0:T(8,128)}), f32[32,8,1,3,130]{4,1,3,2,0:T(8,128)S(1)}, u32[]{:S(2)}, u32[]{:S(2)}) async-start(f32[32,8,1,3,130]{4,1,3,2,0:T(8,128)} %maximum_bitcast_fusion), calls=%async_computation.1 | async-start | bytes 1572864 | tf_op jit(solution)/shard_map/all_to_all | solution.py:155
  64.2 0.1 fusion.55
  64.6 0.3 select_reduce_fusion.1
  64.9 0.1 copy.172
  65.1 12.5 %all-to-all-done.1 = f32[32,8,1,3,130]{4,1,3,2,0:T(8,128)S(1)} async-done(((f32[32,8,1,3,130]{4,1,3,2,0:T(8,128)}), f32[32,8,1,3,130]{4,1,3,2,0:T(8,128)S(1)}, u32[]{:S(2)}, u32[]{:S(2)}) %all-to-all-start.1) | async-done | bytes 399392 | tf_op jit(solution)/shard_map/all_to_all | solution.py:155
  77.5 0.2 fusion.61
  77.7 0.2 copy.185
  78.0 0.2 copy.186
  78.3 0.2 fusion.32
  78.4 0.1 copy.175
  78.5 0.2 fusion.33
  78.7 0.1 copy.179
  78.8 0.1 copy.173
  78.9 0.1 copy.166
  79.0 0.2 fusion.12
  79.2 0.2 fusion.10
  79.5 23.1 %all_gather.10 = bf16[256,384]{1,0:T(8,128)(2,1)S(1)} all-gather(bf16[8,384]{1,0:T(8,128)(2,1)S(1)} %bitcast.108), channel_id=1, replica_groups=mesh['kv'=8,'blk'=32] {'blk'}, dimensions={0}, use_global_device_ids=true | all-gather | bytes 202752 | tf_op jit(solution)/shard_map/all_gather | solution.py:189
  102.6 0.2 fusion.62
  102.8 2.0 collective-permute-start
  104.8 3.3 %collective-permute-done = f32[256,96]{0,1:T(8,128)S(1)} collective-permute-done((f32[256,96]{0,1:T(8,128)S(1)}, f32[256,96]{0,1:T(8,128)S(1)}, u32[]{:S(2)}, u32[]{:S(2)}) %collective-permute-start) | collective-permute-done | bytes 98336 | tf_op jit(solution)/shard_map/ppermute | solution.py:22
  108.1 3.4 %collective-permute-start.1 = (f32[256,96]{0,1:T(8,128)S(1)}, f32[256,96]{0,1:T(8,128)S(1)}, u32[]{:S(2)}, u32[]{:S(2)}) collective-permute-start(f32[256,96]{0,1:T(8,128)S(1)} %add.109), channel_id=1, source_target_pairs={{0,64},{32,96},{64,0},{96,32},{128,192},{160,224},{192,128},{224,1... | collective-permute-start | bytes 294920 | tf_op jit(solution)/shard_map/ppermute | solution.py:22
  111.4 4.8 %collective-permute-done.1 = f32[256,96]{0,1:T(8,128)S(1)} collective-permute-done((f32[256,96]{0,1:T(8,128)S(1)}, f32[256,96]{0,1:T(8,128)S(1)}, u32[]{:S(2)}, u32[]{:S(2)}) %collective-permute-start.1) | collective-permute-done | bytes 98336 | tf_op jit(solution)/shard_map/ppermute | solution.py:22
  116.3 6.3 %collective-permute-start.2 = (f32[256,96]{0,1:T(8,128)S(1)}, f32[256,96]{0,1:T(8,128)S(1)}, u32[]{:S(2)}, u32[]{:S(2)}) collective-permute-start(f32[256,96]{0,1:T(8,128)S(1)} %add.110), channel_id=1, source_target_pairs={{0,128},{32,160},{64,192},{96,224},{128,0},{160,32},{192,64},{224,... | collective-permute-start | bytes 294920 | tf_op jit(solution)/shard_map/ppermute | solution.py:22
  122.5 3.6 %collective-permute-done.2 = f32[256,96]{0,1:T(8,128)S(1)} collective-permute-done((f32[256,96]{0,1:T(8,128)S(1)}, f32[256,96]{0,1:T(8,128)S(1)}, u32[]{:S(2)}, u32[]{:S(2)}) %collective-permute-start.2) | collective-permute-done | bytes 98336 | tf_op jit(solution)/shard_map/ppermute | solution.py:22
  126.2 0.2 concatenate.91
  126.5 0.5 convolution_bitcast_fusion
  127.0 0.2 pad_maximum_fusion
  127.2 34.6 %all_to_all.15 = f32[32,8,2049]{2,1,0:T(8,128)S(1)} all-to-all(f32[32,8,2049]{2,1,0:T(8,128)S(1)} %pad_maximum_fusion), channel_id=1, replica_groups=mesh['kv'=8,'blk'=32] {'blk'}, dimensions={0} | all-to-all | bytes 4196352 | tf_op jit(solution)/shard_map/all_to_all | solution.py:37
  161.8 0.1 reduce_sum.89
  161.9 0.1 fusion.50
  162.0 0.1 fusion.28
  162.1 23.3 %all_gather.11 = bf16[256,1024]{1,0:T(8,128)(2,1)S(1)} all-gather(bf16[8,1024]{1,0:T(8,128)(2,1)S(1)} %fusion.28), channel_id=1, replica_groups=mesh['kv'=8,'blk'=32] {'blk'}, dimensions={0}, use_global_device_ids=true | all-gather | bytes 540672 | tf_op jit(solution)/shard_map/all_gather | solution.py:208
  185.5 0.3 fusion.63
  185.8 0.1 collective-permute-start.3
  185.9 5.0 %collective-permute-done.3 = f32[256,96]{0,1:T(8,128)S(1)} collective-permute-done((f32[256,96]{0,1:T(8,128)S(1)}, f32[256,96]{0,1:T(8,128)S(1)}, u32[]{:S(2)}, u32[]{:S(2)}) %collective-permute-start.3) | collective-permute-done | bytes 98336 | tf_op jit(solution)/shard_map/ppermute | solution.py:22
  190.9 3.3 %collective-permute-start.4 = (f32[256,96]{0,1:T(8,128)S(1)}, f32[256,96]{0,1:T(8,128)S(1)}, u32[]{:S(2)}, u32[]{:S(2)}) collective-permute-start(f32[256,96]{0,1:T(8,128)S(1)} %add.115), channel_id=1, source_target_pairs={{0,64},{32,96},{64,0},{96,32},{128,192},{160,224},{192,128},{224,1... | collective-permute-start | bytes 294920 | tf_op jit(solution)/shard_map/ppermute | solution.py:22
  194.2 4.8 %collective-permute-done.4 = f32[256,96]{0,1:T(8,128)S(1)} collective-permute-done((f32[256,96]{0,1:T(8,128)S(1)}, f32[256,96]{0,1:T(8,128)S(1)}, u32[]{:S(2)}, u32[]{:S(2)}) %collective-permute-start.4) | collective-permute-done | bytes 98336 | tf_op jit(solution)/shard_map/ppermute | solution.py:22
  199.0 4.3 %collective-permute-start.5 = (f32[256,96]{0,1:T(8,128)S(1)}, f32[256,96]{0,1:T(8,128)S(1)}, u32[]{:S(2)}, u32[]{:S(2)}) collective-permute-start(f32[256,96]{0,1:T(8,128)S(1)} %add.116), channel_id=1, source_target_pairs={{0,128},{32,160},{64,192},{96,224},{128,0},{160,32},{192,64},{224,... | collective-permute-start | bytes 294920 | tf_op jit(solution)/shard_map/ppermute | solution.py:22
  203.4 6.2 %collective-permute-done.5 = f32[256,96]{0,1:T(8,128)S(1)} collective-permute-done((f32[256,96]{0,1:T(8,128)S(1)}, f32[256,96]{0,1:T(8,128)S(1)}, u32[]{:S(2)}, u32[]{:S(2)}) %collective-permute-start.5) | collective-permute-done | bytes 98336 | tf_op jit(solution)/shard_map/ppermute | solution.py:22
  209.6 0.7 add_bitcast_fusion
  (71 shorter events, 1.4 us)
Async XLA Ops:
  0.6 48.4 %copy-start = (bf16[8,1,128,128]{3,2,1,0:T(8,128)(2,1)S(1)}, bf16[8,1,128,128]{3,2,1,0:T(8,128)(2,1)}, u32[]{:S(2)}) copy-start(bf16[8,1,128,128]{3,2,1,0:T(8,128)(2,1)} %param.30) | copy-start | bytes 786436
  0.6 11.8 %copy-start.12 = (s32[32]{0:T(128)S(1)}, s32[32]{0:T(128)}, u32[]{:S(2)}) copy-start(s32[32]{0:T(128)} %param.35) | copy-start | bytes 388
  0.7 12.0 %copy-start.14 = (s32[8]{0:T(128)S(1)}, s32[8]{0:T(128)}, u32[]{:S(2)}) copy-start(s32[8]{0:T(128)} %param.37) | copy-start | bytes 100
  0.7 12.0 %copy-start.15 = (s32[1,8]{1,0:T(1,128)S(1)}, s32[1,8]{1,0:T(1,128)}, u32[]{:S(2)}) copy-start(s32[1,8]{1,0:T(1,128)} %param.34) | copy-start | bytes 100
  0.7 12.1 %copy-start.6 = (bf16[8,1,127,128]{3,0,2,1:T(8,128)(2,1)S(1)}, bf16[8,1,127,128]{3,0,2,1:T(8,128)(2,1)}, u32[]{:S(2)}) copy-start(bf16[8,1,127,128]{3,0,2,1:T(8,128)(2,1)} %param.32) | copy-start | bytes 780292
  0.7 12.1 %copy-start.7 = (bf16[8,1,127,128]{3,0,2,1:T(8,128)(2,1)S(1)}, bf16[8,1,127,128]{3,0,2,1:T(8,128)(2,1)}, u32[]{:S(2)}) copy-start(bf16[8,1,127,128]{3,0,2,1:T(8,128)(2,1)} %param.33) | copy-start | bytes 780292
  2.7 10.5 %copy-start.16 = (s32[5]{0:T(128)S(1)}, s32[5]{0:T(128)}, u32[]{:S(2)}) copy-start(s32[5]{0:T(128)} %param.36) | copy-start | bytes 64
  4.8 20.9 %all-to-all-start = ((f32[32,8,641]{2,1,0:T(8,128)}), f32[32,8,641]{2,1,0:T(8,128)S(1)}, u32[]{:S(2)}, u32[]{:S(2)}) async-start(f32[32,8,641]{2,1,0:T(8,128)} %pad_maximum_fusion.1), calls=%async_computation | async-start | bytes 1572864 | tf_op jit(solution)/shard_map/all_to_all | solution.py:37
  54.7 9.7 %copy-start.1 = (bf16[8,1,128,128]{3,2,0,1:T(8,128)(2,1)S(1)}, bf16[8,1,128,128]{3,2,0,1:T(8,128)(2,1)}, u32[]{:S(2)}) copy-start(bf16[8,1,128,128]{3,2,0,1:T(8,128)(2,1)} %get-tuple-element.66) | copy-start | bytes 786436
  55.4 9.6 %copy-start.4 = (bf16[8,1,128,128]{3,2,0,1:T(8,128)(2,1)S(1)}, bf16[8,1,128,128]{3,2,0,1:T(8,128)(2,1)}, u32[]{:S(2)}) copy-start(bf16[8,1,128,128]{3,2,0,1:T(8,128)(2,1)} %get-tuple-element.67) | copy-start | bytes 786436
  58.5 44.1 %copy-start.11 = (bf16[384,96]{0,1:T(8,128)(2,1)S(1)}, bf16[384,96]{0,1:T(8,128)(2,1)}, u32[]{:S(2)}) copy-start(bf16[384,96]{0,1:T(8,128)(2,1)} %param.25) | copy-start | bytes 221188
  58.5 67.7 %copy-start.3 = (bf16[1,256,96]{1,2,0:T(8,128)(2,1)S(1)}, bf16[1,256,96]{1,2,0:T(8,128)(2,1)}, u32[]{:S(2)}) copy-start(bf16[1,256,96]{1,2,0:T(8,128)(2,1)} %param.22) | copy-start | bytes 147460
  58.5 68.0 %copy-start.8 = (bf16[96,1024]{1,0:T(8,128)(2,1)S(1)}, bf16[96,1024]{1,0:T(8,128)(2,1)}, u32[]{:S(2)}) copy-start(bf16[96,1024]{1,0:T(8,128)(2,1)} %param.28) | copy-start | bytes 589828
  58.5 68.0 %copy-start.9 = (bf16[96,1024]{1,0:T(8,128)(2,1)S(1)}, bf16[96,1024]{1,0:T(8,128)(2,1)}, u32[]{:S(2)}) copy-start(bf16[96,1024]{1,0:T(8,128)(2,1)} %param.27) | copy-start | bytes 589828
  58.5 68.0 %copy-start.13 = (f32[96]{0:T(128)S(1)}, f32[96]{0:T(128)}, u32[]{:S(2)}) copy-start(f32[96]{0:T(128)} %param.26) | copy-start | bytes 1156
  58.5 19.0 %all-to-all-start.1 = ((f32[32,8,1,3,130]{4,1,3,2,0:T(8,128)}), f32[32,8,1,3,130]{4,1,3,2,0:T(8,128)S(1)}, u32[]{:S(2)}, u32[]{:S(2)}) async-start(f32[32,8,1,3,130]{4,1,3,2,0:T(8,128)} %maximum_bitcast_fusion), calls=%async_computation.1 | async-start | bytes 1572864 | tf_op jit(solution)/shard_map/all_to_all | solution.py:155
  64.5 62.5 %copy-start.2 = (bf16[8,1,128,128]{3,2,0,1:T(8,128)(2,1)}, bf16[8,1,128,128]{3,2,0,1:T(8,128)(2,1)S(1)}, u32[]{:S(2)}) copy-start(bf16[8,1,128,128]{3,2,0,1:T(8,128)(2,1)S(1)} %scatter.6) | copy-start | bytes 786436
  65.0 62.0 %copy-start.5 = (bf16[8,1,128,128]{3,2,0,1:T(8,128)(2,1)}, bf16[8,1,128,128]{3,2,0,1:T(8,128)(2,1)S(1)}, u32[]{:S(2)}) copy-start(bf16[8,1,128,128]{3,2,0,1:T(8,128)(2,1)S(1)} %scatter.9) | copy-start | bytes 786436
  102.8 5.3 %collective-permute-start = (f32[256,96]{0,1:T(8,128)S(1)}, f32[256,96]{0,1:T(8,128)S(1)}, u32[]{:S(2)}, u32[]{:S(2)}) collective-permute-start(f32[256,96]{0,1:T(8,128)S(1)} %fusion.62), channel_id=1, source_target_pairs={{0,32},{32,0},{64,96},{96,64},{128,160},{160,128},{192,224},{224,1... | collective-permute-start | bytes 294920 | tf_op jit(solution)/shard_map/ppermute | solution.py:22
  108.1 8.2 %collective-permute-start.1 = (f32[256,96]{0,1:T(8,128)S(1)}, f32[256,96]{0,1:T(8,128)S(1)}, u32[]{:S(2)}, u32[]{:S(2)}) collective-permute-start(f32[256,96]{0,1:T(8,128)S(1)} %add.109), channel_id=1, source_target_pairs={{0,64},{32,96},{64,0},{96,32},{128,192},{160,224},{192,128},{224,1... | collective-permute-start | bytes 294920 | tf_op jit(solution)/shard_map/ppermute | solution.py:22
  116.3 9.9 %collective-permute-start.2 = (f32[256,96]{0,1:T(8,128)S(1)}, f32[256,96]{0,1:T(8,128)S(1)}, u32[]{:S(2)}, u32[]{:S(2)}) collective-permute-start(f32[256,96]{0,1:T(8,128)S(1)} %add.110), channel_id=1, source_target_pairs={{0,128},{32,160},{64,192},{96,224},{128,0},{160,32},{192,64},{224,... | collective-permute-start | bytes 294920 | tf_op jit(solution)/shard_map/ppermute | solution.py:22
  127.2 58.3 %copy-start.10 = (bf16[1024,96]{0,1:T(8,128)(2,1)S(1)}, bf16[1024,96]{0,1:T(8,128)(2,1)}, u32[]{:S(2)}) copy-start(bf16[1024,96]{0,1:T(8,128)(2,1)} %param.29) | copy-start | bytes 589828
  185.8 5.1 %collective-permute-start.3 = (f32[256,96]{0,1:T(8,128)S(1)}, f32[256,96]{0,1:T(8,128)S(1)}, u32[]{:S(2)}, u32[]{:S(2)}) collective-permute-start(f32[256,96]{0,1:T(8,128)S(1)} %fusion.63), channel_id=1, source_target_pairs={{0,32},{32,0},{64,96},{96,64},{128,160},{160,128},{192,224},{224,1... | collective-permute-start | bytes 294920 | tf_op jit(solution)/shard_map/ppermute | solution.py:22
  190.9 8.1 %collective-permute-start.4 = (f32[256,96]{0,1:T(8,128)S(1)}, f32[256,96]{0,1:T(8,128)S(1)}, u32[]{:S(2)}, u32[]{:S(2)}) collective-permute-start(f32[256,96]{0,1:T(8,128)S(1)} %add.115), channel_id=1, source_target_pairs={{0,64},{32,96},{64,0},{96,32},{128,192},{160,224},{192,128},{224,1... | collective-permute-start | bytes 294920 | tf_op jit(solution)/shard_map/ppermute | solution.py:22
  199.0 10.6 %collective-permute-start.5 = (f32[256,96]{0,1:T(8,128)S(1)}, f32[256,96]{0,1:T(8,128)S(1)}, u32[]{:S(2)}, u32[]{:S(2)}) collective-permute-start(f32[256,96]{0,1:T(8,128)S(1)} %add.116), channel_id=1, source_target_pairs={{0,128},{32,160},{64,192},{96,224},{128,0},{160,32},{192,64},{224,... | collective-permute-start | bytes 294920 | tf_op jit(solution)/shard_map/ppermute | solution.py:22
where the time goes:
time: 211 us; the launch traced here: 210 us
  blocking collectives  104 us (49%)
  waiting for transfers between devices  49.7 us (24%)
  starting transfers between devices  32.7 us (15%)
  other arithmetic  10.9 us (5%)
  matrix products  6.5 us (3%)
  local copies, waits for them, and re-layouts  5.57 us (3%)
    all_to_all x1, blocking collectives, scatter_sum(): return jnp.sum(lax.all_to_all(pieces, axis, 0, 0, tiled=False), axis=0)  34.6 us
    ppermute x6, waiting for transfers between devices, exchange(): return lax.ppermute(value, axis, [(i, i ^ 1 << bit) for i in range(count)])  27.9 us
    all_gather x1, blocking collectives, body(): lax.all_gather(hidden, 'blk', axis=0, tiled=True)  23.3 us
    all_gather x1, blocking collectives, body(): lax.all_gather(heads_out, 'blk', axis=0, tiled=True)  23.1 us
    all_gather x1, blocking collectives, body(): query_rows = lax.all_gather(own_queries, 'blk', axis=0, tiled=True)  22.9 us
    ppermute x6, starting transfers between devices, exchange(): return lax.ppermute(value, axis, [(i, i ^ 1 << bit) for i in range(count)])  19.3 us
    all_to_all x1, waiting for transfers between devices, body(): parts = lax.all_to_all(packed, 'blk', 0, 0, tiled=False)  12.5 us
    all_to_all x1, waiting for transfers between devices, scatter_sum(): return jnp.sum(lax.all_to_all(pieces, axis, 0, 0, tiled=False), axis=0)  9.32 us
  transfers between devices with their start and end apart: 8, of which 8 were waited for; matrix products, arithmetic and copies ran while one was open for 2% of the time, Pallas kernels for 0%

commit v1 on v0

--- a/solution.py
+++ b/solution.py
@@ -123,7 +123,9 @@
     own_queries = rotate(own_proj[:, :, :group_queries], own_angle[:, None, None, :]).astype(
         jnp.bfloat16
     )
-    query_rows = lax.all_gather(own_queries, "blk", axis=0, tiled=True)
+    query_rows = jnp.concatenate(
+        lax.all_to_all(jnp.stack([own_queries] * lax.axis_size("blk")), "blk", 0, 0), axis=0
+    )
     new_key = rotate(own_proj[:, :, group_queries], own_angle[:, None, :]).astype(jnp.bfloat16)
     new_value = own_proj[:, :, group_queries + 1].astype(jnp.bfloat16)
     parent_rows = base_rows + parents[0]

time: 211 us -> 201 us (0.953)
  blocking collectives: 104 us -> 81 us
  waiting for transfers between devices: 49.7 us -> 56.9 us
  starting transfers between devices: 32.7 us -> 37.2 us
    all_gather x1 -> x0, blocking collectives: 22.9 us -> none  [body(): query_rows = lax.all_gather(own_queries, 'blk', axis=0, tiled=True)]
    all_to_all x0 -> x1, waiting for transfers between devices: none -> 7.09 us  [body(): lax.all_to_all(jnp.stack([own_queries] * lax.axis_size('blk')), 'blk', 0, 0)]
    all_to_all x0 -> x1, starting transfers between devices: none -> 5.01 us  [body(): lax.all_to_all(jnp.stack([own_queries] * lax.axis_size('blk')), 'blk', 0, 0)]
  transfers between devices with their start and end apart: 8 -> 9, of which waited for: 8 -> 9; matrix products, arithmetic and copies ran while one was open for 2% -> 2% of each run, Pallas kernels for 0% -> 0%
where the time goes in v1:
time: 201 us
  blocking collectives  81 us (40%)
  waiting for transfers between devices  56.9 us (28%)
  starting transfers between devices  37.2 us (19%)
  other arithmetic  10.9 us (5%)
  local copies, waits for them, and re-layouts  7 us (3%)
  matrix products  6.61 us (3%)
    all_to_all x1, blocking collectives, scatter_sum(): return jnp.sum(lax.all_to_all(pieces, axis, 0, 0, tiled=False), axis=0)  34.6 us
    ppermute x6, waiting for transfers between devices, exchange(): return lax.ppermute(value, axis, [(i, i ^ 1 << bit) for i in range(count)])  27.9 us
    all_gather x1, blocking collectives, body(): lax.all_gather(hidden, 'blk', axis=0, tiled=True)  23.3 us
    all_gather x1, blocking collectives, body(): lax.all_gather(heads_out, 'blk', axis=0, tiled=True)  23.1 us
    ppermute x6, starting transfers between devices, exchange(): return lax.ppermute(value, axis, [(i, i ^ 1 << bit) for i in range(count)])  19.3 us
    all_to_all x1, waiting for transfers between devices, body(): parts = lax.all_to_all(packed, 'blk', 0, 0, tiled=False)  12.6 us
    all_to_all x1, waiting for transfers between devices, scatter_sum(): return jnp.sum(lax.all_to_all(pieces, axis, 0, 0, tiled=False), axis=0)  9.32 us
    all_to_all x1, starting transfers between devices, scatter_sum(): return jnp.sum(lax.all_to_all(pieces, axis, 0, 0, tiled=False), axis=0)  7.62 us
  transfers between devices with their start and end apart: 9, of which 9 were waited for; matrix products, arithmetic and copies ran while one was open for 2% of the time, Pallas kernels for 0%

profile of v1, /device:TPU:2, one launch (start us, length us, event | category | flops | bytes accessed | tf_op | source)
XLA Modules:
  0.0 200.7 jit_solution(7584566865924731231)
XLA Ops:
  0.7 1.0 copy.175
  1.7 0.8 fusion.24
  2.5 0.2 concatenate.85
  2.7 1.1 fusion.22
  3.9 0.9 pad_maximum_fusion.1
  4.8 7.6 %all-to-all-start = ((f32[32,8,641]{2,1,0:T(8,128)}), f32[32,8,641]{2,1,0:T(8,128)S(1)}, u32[]{:S(2)}, u32[]{:S(2)}) async-start(f32[32,8,641]{2,1,0:T(8,128)} %pad_maximum_fusion.1), calls=%async_computation | async-start | bytes 1572864 | tf_op jit(solution)/shard_map/all_to_all | solution.py:37
  12.6 0.1 lt.33
  13.0 0.1 multiply_cosine_fusion.1
  13.3 0.6 gather_fusion
  13.9 0.6 gather_fusion.1
  14.5 0.1 convert_reduce_fusion
  14.6 1.0 compare_and_fusion
  15.6 0.9 bitcast_select_fusion.1
  16.5 9.3 %all-to-all-done = f32[32,8,641]{2,1,0:T(8,128)S(1)} async-done(((f32[32,8,641]{2,1,0:T(8,128)}), f32[32,8,641]{2,1,0:T(8,128)S(1)}, u32[]{:S(2)}, u32[]{:S(2)}) %all-to-all-start) | async-done | bytes 656416 | tf_op jit(solution)/shard_map/all_to_all | solution.py:37
  25.8 0.1 fusion.59
  26.2 0.7 stack.4
  26.9 5.0 %all-to-all-start.1 = ((bf16[32,8,1,3,128]{4,1,3,2,0:T(8,128)(2,1)}), bf16[32,8,1,3,128]{4,1,3,2,0:T(8,128)(2,1)S(1)}, u32[]{:S(2)}, u32[]{:S(2)}) async-start(bf16[32,8,1,3,128]{4,1,3,2,0:T(8,128)(2,1)} %stack.4), calls=%async_computation.1 | async-start | bytes 393216 | tf_op jit(solution)/shard_map/all_to_all | solution.py:127
  32.0 7.1 %all-to-all-done.1 = bf16[32,8,1,3,128]{4,1,3,2,0:T(8,128)(2,1)S(1)} async-done(((bf16[32,8,1,3,128]{4,1,3,2,0:T(8,128)(2,1)}), bf16[32,8,1,3,128]{4,1,3,2,0:T(8,128)(2,1)S(1)}, u32[]{:S(2)}, u32[]{:S(2)}) %all-to-all-start.1) | async-done | bytes 196640 | tf_op jit(solution)/shard_map/all_to_all | solution.py:127
  39.0 0.7 copy-done.3
  39.7 1.9 select_reduce_fusion
  41.6 0.1 concatenate.73
  41.7 3.1 %fusion.2 = (bf16[32,8,3,1024]{3,1,0,2:T(8,128)(2,1)}, f32[256,3]{0,1:T(4,128)S(1)}) fusion(f32[256,3,1024]{2,0,1:T(8,128)S(1)} %get-tuple-element.73, f32[256,3]{0,1:T(4,128)S(1)} %get-tuple-element.72, pred[256,1024]{1,0:T(8,128)(4,1)} %compare_and_fusion), kind=kLoop, calls=%fused_computation.8 | loop fusion | flops 3931392 | bytes 4986880 | tf_op jit(solution)/shard_map/reshape.476
  44.8 0.1 concatenate.74
  44.9 0.6 copy.183
  45.5 0.6 copy.182
  46.2 2.0 %fusion.5 = f32[32,8,1,3,128]{4,1,3,0,2:T(8,128)S(1)} fusion(bf16[1024,128,1,1]{1,0,3,2:T(8,128)(2,1)} %bitcast.110, bf16[32,8,3,1024]{3,1,0,2:T(8,128)(2,1)} %get-tuple-element.55), kind=kOutput, calls=%fused_computation.11 | convolution fusion | flops 201326592 | bytes 2228224 | tf_op jit(solution)/shard_map/kqn,knd->kqd/dot_general | solution.py:149
  48.2 1.1 maximum_bitcast_fusion
  49.3 5.2 %all-to-all-start.2 = ((f32[32,8,1,3,130]{4,1,3,2,0:T(8,128)}), f32[32,8,1,3,130]{4,1,3,2,0:T(8,128)S(1)}, u32[]{:S(2)}, u32[]{:S(2)}) async-start(f32[32,8,1,3,130]{4,1,3,2,0:T(8,128)} %maximum_bitcast_fusion), calls=%async_computation.2 | async-start | bytes 1572864 | tf_op jit(solution)/shard_map/all_to_all | solution.py:157
  54.5 0.1 fusion.61
  54.8 0.3 select_reduce_fusion.1
  55.1 0.1 copy.191
  55.3 12.6 %all-to-all-done.2 = f32[32,8,1,3,130]{4,1,3,2,0:T(8,128)S(1)} async-done(((f32[32,8,1,3,130]{4,1,3,2,0:T(8,128)}), f32[32,8,1,3,130]{4,1,3,2,0:T(8,128)S(1)}, u32[]{:S(2)}, u32[]{:S(2)}) %all-to-all-start.2) | async-done | bytes 399392 | tf_op jit(solution)/shard_map/all_to_all | solution.py:157
  67.9 0.2 fusion.67
  68.1 0.2 copy.206
  68.3 0.2 copy.207
  68.6 0.2 fusion.37
  68.9 0.2 fusion.38
  69.3 0.1 copy.186
  69.4 0.2 fusion.12
  69.6 0.2 fusion.10
  69.8 23.1 %all_gather.6 = bf16[256,384]{1,0:T(8,128)(2,1)S(1)} all-gather(bf16[8,384]{1,0:T(8,128)(2,1)S(1)} %bitcast.109), channel_id=1, replica_groups=mesh['kv'=8,'blk'=32] {'blk'}, dimensions={0}, use_global_device_ids=true | all-gather | bytes 202752 | tf_op jit(solution)/shard_map/all_gather | solution.py:191
  92.9 0.2 fusion.69
  93.1 2.0 collective-permute-start
  95.1 3.3 %collective-permute-done = f32[256,96]{0,1:T(8,128)S(1)} collective-permute-done((f32[256,96]{0,1:T(8,128)S(1)}, f32[256,96]{0,1:T(8,128)S(1)}, u32[]{:S(2)}, u32[]{:S(2)}) %collective-permute-start) | collective-permute-done | bytes 98336 | tf_op jit(solution)/shard_map/ppermute | solution.py:22
  98.5 3.4 %collective-permute-start.1 = (f32[256,96]{0,1:T(8,128)S(1)}, f32[256,96]{0,1:T(8,128)S(1)}, u32[]{:S(2)}, u32[]{:S(2)}) collective-permute-start(f32[256,96]{0,1:T(8,128)S(1)} %add.109), channel_id=1, source_target_pairs={{0,64},{32,96},{64,0},{96,32},{128,192},{160,224},{192,128},{224,1... | collective-permute-start | bytes 294920 | tf_op jit(solution)/shard_map/ppermute | solution.py:22
  101.8 4.8 %collective-permute-done.1 = f32[256,96]{0,1:T(8,128)S(1)} collective-permute-done((f32[256,96]{0,1:T(8,128)S(1)}, f32[256,96]{0,1:T(8,128)S(1)}, u32[]{:S(2)}, u32[]{:S(2)}) %collective-permute-start.1) | collective-permute-done | bytes 98336 | tf_op jit(solution)/shard_map/ppermute | solution.py:22
  106.6 6.3 %collective-permute-start.2 = (f32[256,96]{0,1:T(8,128)S(1)}, f32[256,96]{0,1:T(8,128)S(1)}, u32[]{:S(2)}, u32[]{:S(2)}) collective-permute-start(f32[256,96]{0,1:T(8,128)S(1)} %add.110), channel_id=1, source_target_pairs={{0,128},{32,160},{64,192},{96,224},{128,0},{160,32},{192,64},{224,... | collective-permute-start | bytes 294920 | tf_op jit(solution)/shard_map/ppermute | solution.py:22
  112.9 3.6 %collective-permute-done.2 = f32[256,96]{0,1:T(8,128)S(1)} collective-permute-done((f32[256,96]{0,1:T(8,128)S(1)}, f32[256,96]{0,1:T(8,128)S(1)}, u32[]{:S(2)}, u32[]{:S(2)}) %collective-permute-start.2) | collective-permute-done | bytes 98336 | tf_op jit(solution)/shard_map/ppermute | solution.py:22
  116.6 0.2 concatenate.86
  116.8 0.5 convolution_bitcast_fusion
  117.4 0.2 pad_maximum_fusion
  117.6 34.6 %all_to_all.20 = f32[32,8,2049]{2,1,0:T(8,128)S(1)} all-to-all(f32[32,8,2049]{2,1,0:T(8,128)S(1)} %pad_maximum_fusion), channel_id=1, replica_groups=mesh['kv'=8,'blk'=32] {'blk'}, dimensions={0} | all-to-all | bytes 4196352 | tf_op jit(solution)/shard_map/all_to_all | solution.py:37
  152.2 0.1 reduce_sum.89
  152.3 0.1 fusion.56
  152.4 0.1 fusion.29
  152.5 23.3 %all_gather.7 = bf16[256,1024]{1,0:T(8,128)(2,1)S(1)} all-gather(bf16[8,1024]{1,0:T(8,128)(2,1)S(1)} %fusion.29), channel_id=1, replica_groups=mesh['kv'=8,'blk'=32] {'blk'}, dimensions={0}, use_global_device_ids=true | all-gather | bytes 540672 | tf_op jit(solution)/shard_map/all_gather | solution.py:210
  175.8 0.3 fusion.70
  176.1 0.1 collective-permute-start.3
  176.2 5.0 %collective-permute-done.3 = f32[256,96]{0,1:T(8,128)S(1)} collective-permute-done((f32[256,96]{0,1:T(8,128)S(1)}, f32[256,96]{0,1:T(8,128)S(1)}, u32[]{:S(2)}, u32[]{:S(2)}) %collective-permute-start.3) | collective-permute-done | bytes 98336 | tf_op jit(solution)/shard_map/ppermute | solution.py:22
  181.3 3.3 %collective-permute-start.4 = (f32[256,96]{0,1:T(8,128)S(1)}, f32[256,96]{0,1:T(8,128)S(1)}, u32[]{:S(2)}, u32[]{:S(2)}) collective-permute-start(f32[256,96]{0,1:T(8,128)S(1)} %add.115), channel_id=1, source_target_pairs={{0,64},{32,96},{64,0},{96,32},{128,192},{160,224},{192,128},{224,1... | collective-permute-start | bytes 294920 | tf_op jit(solution)/shard_map/ppermute | solution.py:22
  184.6 4.8 %collective-permute-done.4 = f32[256,96]{0,1:T(8,128)S(1)} collective-permute-done((f32[256,96]{0,1:T(8,128)S(1)}, f32[256,96]{0,1:T(8,128)S(1)}, u32[]{:S(2)}, u32[]{:S(2)}) %collective-permute-start.4) | collective-permute-done | bytes 98336 | tf_op jit(solution)/shard_map/ppermute | solution.py:22
  189.4 4.3 %collective-permute-start.5 = (f32[256,96]{0,1:T(8,128)S(1)}, f32[256,96]{0,1:T(8,128)S(1)}, u32[]{:S(2)}, u32[]{:S(2)}) collective-permute-start(f32[256,96]{0,1:T(8,128)S(1)} %add.116), channel_id=1, source_target_pairs={{0,128},{32,160},{64,192},{96,224},{128,0},{160,32},{192,64},{224,... | collective-permute-start | bytes 294920 | tf_op jit(solution)/shard_map/ppermute | solution.py:22
  193.8 6.2 %collective-permute-done.5 = f32[256,96]{0,1:T(8,128)S(1)} collective-permute-done((f32[256,96]{0,1:T(8,128)S(1)}, f32[256,96]{0,1:T(8,128)S(1)}, u32[]{:S(2)}, u32[]{:S(2)}) %collective-permute-start.5) | collective-permute-done | bytes 98336 | tf_op jit(solution)/shard_map/ppermute | solution.py:22
  200.0 0.7 add_bitcast_fusion
  (76 shorter events, 1.6 us)
Async XLA Ops:
  0.6 39.1 %copy-start = (bf16[8,1,128,128]{3,2,1,0:T(8,128)(2,1)S(1)}, bf16[8,1,128,128]{3,2,1,0:T(8,128)(2,1)}, u32[]{:S(2)}) copy-start(bf16[8,1,128,128]{3,2,1,0:T(8,128)(2,1)} %param.30) | copy-start | bytes 786436
  0.6 11.9 %copy-start.13 = (s32[32]{0:T(128)S(1)}, s32[32]{0:T(128)}, u32[]{:S(2)}) copy-start(s32[32]{0:T(128)} %param.35) | copy-start | bytes 388
  0.7 12.0 %copy-start.15 = (s32[8]{0:T(128)S(1)}, s32[8]{0:T(128)}, u32[]{:S(2)}) copy-start(s32[8]{0:T(128)} %param.37) | copy-start | bytes 100
  0.7 12.0 %copy-start.16 = (s32[1,8]{1,0:T(1,128)S(1)}, s32[1,8]{1,0:T(1,128)}, u32[]{:S(2)}) copy-start(s32[1,8]{1,0:T(1,128)} %param.34) | copy-start | bytes 100
  0.7 12.1 %copy-start.7 = (bf16[8,1,127,128]{3,0,2,1:T(8,128)(2,1)S(1)}, bf16[8,1,127,128]{3,0,2,1:T(8,128)(2,1)}, u32[]{:S(2)}) copy-start(bf16[8,1,127,128]{3,0,2,1:T(8,128)(2,1)} %param.32) | copy-start | bytes 780292
  0.7 12.2 %copy-start.8 = (bf16[8,1,127,128]{3,0,2,1:T(8,128)(2,1)S(1)}, bf16[8,1,127,128]{3,0,2,1:T(8,128)(2,1)}, u32[]{:S(2)}) copy-start(bf16[8,1,127,128]{3,0,2,1:T(8,128)(2,1)} %param.33) | copy-start | bytes 780292
  2.7 10.5 %copy-start.17 = (s32[5]{0:T(128)S(1)}, s32[5]{0:T(128)}, u32[]{:S(2)}) copy-start(s32[5]{0:T(128)} %param.36) | copy-start | bytes 64
  4.8 20.9 %all-to-all-start = ((f32[32,8,641]{2,1,0:T(8,128)}), f32[32,8,641]{2,1,0:T(8,128)S(1)}, u32[]{:S(2)}, u32[]{:S(2)}) async-start(f32[32,8,641]{2,1,0:T(8,128)} %pad_maximum_fusion.1), calls=%async_computation | async-start | bytes 1572864 | tf_op jit(solution)/shard_map/all_to_all | solution.py:37
  26.9 12.1 %all-to-all-start.1 = ((bf16[32,8,1,3,128]{4,1,3,2,0:T(8,128)(2,1)}), bf16[32,8,1,3,128]{4,1,3,2,0:T(8,128)(2,1)S(1)}, u32[]{:S(2)}, u32[]{:S(2)}) async-start(bf16[32,8,1,3,128]{4,1,3,2,0:T(8,128)(2,1)} %stack.4), calls=%async_computation.1 | async-start | bytes 393216 | tf_op jit(solution)/shard_map/all_to_all | solution.py:127
  39.0 0.7 copy-start.3
  45.5 9.2 %copy-start.1 = (bf16[8,1,128,128]{3,2,0,1:T(8,128)(2,1)S(1)}, bf16[8,1,128,128]{3,2,0,1:T(8,128)(2,1)}, u32[]{:S(2)}) copy-start(bf16[8,1,128,128]{3,2,0,1:T(8,128)(2,1)} %get-tuple-element.68) | copy-start | bytes 786436
  46.2 9.1 %copy-start.5 = (bf16[8,1,128,128]{3,2,0,1:T(8,128)(2,1)S(1)}, bf16[8,1,128,128]{3,2,0,1:T(8,128)(2,1)}, u32[]{:S(2)}) copy-start(bf16[8,1,128,128]{3,2,0,1:T(8,128)(2,1)} %get-tuple-element.69) | copy-start | bytes 786436
  49.3 43.6 %copy-start.12 = (bf16[384,96]{0,1:T(8,128)(2,1)S(1)}, bf16[384,96]{0,1:T(8,128)(2,1)}, u32[]{:S(2)}) copy-start(bf16[384,96]{0,1:T(8,128)(2,1)} %param.25) | copy-start | bytes 221188
  49.3 67.3 %copy-start.4 = (bf16[1,256,96]{1,2,0:T(8,128)(2,1)S(1)}, bf16[1,256,96]{1,2,0:T(8,128)(2,1)}, u32[]{:S(2)}) copy-start(bf16[1,256,96]{1,2,0:T(8,128)(2,1)} %param.22) | copy-start | bytes 147460
  49.3 67.5 %copy-start.9 = (bf16[96,1024]{1,0:T(8,128)(2,1)S(1)}, bf16[96,1024]{1,0:T(8,128)(2,1)}, u32[]{:S(2)}) copy-start(bf16[96,1024]{1,0:T(8,128)(2,1)} %param.28) | copy-start | bytes 589828
  49.3 67.5 %copy-start.10 = (bf16[96,1024]{1,0:T(8,128)(2,1)S(1)}, bf16[96,1024]{1,0:T(8,128)(2,1)}, u32[]{:S(2)}) copy-start(bf16[96,1024]{1,0:T(8,128)(2,1)} %param.27) | copy-start | bytes 589828
  49.3 67.5 %copy-start.14 = (f32[96]{0:T(128)S(1)}, f32[96]{0:T(128)}, u32[]{:S(2)}) copy-start(f32[96]{0:T(128)} %param.26) | copy-start | bytes 1156
  49.3 18.6 %all-to-all-start.2 = ((f32[32,8,1,3,130]{4,1,3,2,0:T(8,128)}), f32[32,8,1,3,130]{4,1,3,2,0:T(8,128)S(1)}, u32[]{:S(2)}, u32[]{:S(2)}) async-start(f32[32,8,1,3,130]{4,1,3,2,0:T(8,128)} %maximum_bitcast_fusion), calls=%async_computation.2 | async-start | bytes 1572864 | tf_op jit(solution)/shard_map/all_to_all | solution.py:157
  54.8 62.5 %copy-start.2 = (bf16[8,1,128,128]{3,2,0,1:T(8,128)(2,1)}, bf16[8,1,128,128]{3,2,0,1:T(8,128)(2,1)S(1)}, u32[]{:S(2)}) copy-start(bf16[8,1,128,128]{3,2,0,1:T(8,128)(2,1)S(1)} %scatter.6) | copy-start | bytes 786436
  55.3 62.1 %copy-start.6 = (bf16[8,1,128,128]{3,2,0,1:T(8,128)(2,1)}, bf16[8,1,128,128]{3,2,0,1:T(8,128)(2,1)S(1)}, u32[]{:S(2)}) copy-start(bf16[8,1,128,128]{3,2,0,1:T(8,128)(2,1)S(1)} %scatter.9) | copy-start | bytes 786436
  93.1 5.3 %collective-permute-start = (f32[256,96]{0,1:T(8,128)S(1)}, f32[256,96]{0,1:T(8,128)S(1)}, u32[]{:S(2)}, u32[]{:S(2)}) collective-permute-start(f32[256,96]{0,1:T(8,128)S(1)} %fusion.69), channel_id=1, source_target_pairs={{0,32},{32,0},{64,96},{96,64},{128,160},{160,128},{192,224},{224,1... | collective-permute-start | bytes 294920 | tf_op jit(solution)/shard_map/ppermute | solution.py:22
  98.5 8.2 %collective-permute-start.1 = (f32[256,96]{0,1:T(8,128)S(1)}, f32[256,96]{0,1:T(8,128)S(1)}, u32[]{:S(2)}, u32[]{:S(2)}) collective-permute-start(f32[256,96]{0,1:T(8,128)S(1)} %add.109), channel_id=1, source_target_pairs={{0,64},{32,96},{64,0},{96,32},{128,192},{160,224},{192,128},{224,1... | collective-permute-start | bytes 294920 | tf_op jit(solution)/shard_map/ppermute | solution.py:22
  106.6 9.9 %collective-permute-start.2 = (f32[256,96]{0,1:T(8,128)S(1)}, f32[256,96]{0,1:T(8,128)S(1)}, u32[]{:S(2)}, u32[]{:S(2)}) collective-permute-start(f32[256,96]{0,1:T(8,128)S(1)} %add.110), channel_id=1, source_target_pairs={{0,128},{32,160},{64,192},{96,224},{128,0},{160,32},{192,64},{224,... | collective-permute-start | bytes 294920 | tf_op jit(solution)/shard_map/ppermute | solution.py:22
  117.6 58.3 %copy-start.11 = (bf16[1024,96]{0,1:T(8,128)(2,1)S(1)}, bf16[1024,96]{0,1:T(8,128)(2,1)}, u32[]{:S(2)}) copy-start(bf16[1024,96]{0,1:T(8,128)(2,1)} %param.29) | copy-start | bytes 589828
  176.1 5.1 %collective-permute-start.3 = (f32[256,96]{0,1:T(8,128)S(1)}, f32[256,96]{0,1:T(8,128)S(1)}, u32[]{:S(2)}, u32[]{:S(2)}) collective-permute-start(f32[256,96]{0,1:T(8,128)S(1)} %fusion.70), channel_id=1, source_target_pairs={{0,32},{32,0},{64,96},{96,64},{128,160},{160,128},{192,224},{224,1... | collective-permute-start | bytes 294920 | tf_op jit(solution)/shard_map/ppermute | solution.py:22
  181.3 8.1 %collective-permute-start.4 = (f32[256,96]{0,1:T(8,128)S(1)}, f32[256,96]{0,1:T(8,128)S(1)}, u32[]{:S(2)}, u32[]{:S(2)}) collective-permute-start(f32[256,96]{0,1:T(8,128)S(1)} %add.115), channel_id=1, source_target_pairs={{0,64},{32,96},{64,0},{96,32},{128,192},{160,224},{192,128},{224,1... | collective-permute-start | bytes 294920 | tf_op jit(solution)/shard_map/ppermute | solution.py:22
  189.4 10.6 %collective-permute-start.5 = (f32[256,96]{0,1:T(8,128)S(1)}, f32[256,96]{0,1:T(8,128)S(1)}, u32[]{:S(2)}, u32[]{:S(2)}) collective-permute-start(f32[256,96]{0,1:T(8,128)S(1)} %add.116), channel_id=1, source_target_pairs={{0,128},{32,160},{64,192},{96,224},{128,0},{160,32},{192,64},{224,... | collective-permute-start | bytes 294920 | tf_op jit(solution)/shard_map/ppermute | solution.py:22
